TPU v7x, 256 devices: a whole 4x4x8 slice. The times are simulated.
256 devices in a mesh: var: 8 (over y, core), tok: 32 (over x, z).
Axes of the slice: x: 4, y: 4, z: 8, core: 2. Of those that a mesh axis runs over, the one named last changes fastest.
Arguments:
- patches: bfloat16 [72, 4, 4096], P('var', None, 'tok'), may hold values from -6 to 6
- slot_var: int32 [72], replicated, may hold values from -1 to 47, as said below
- patch_weight: bfloat16 [48, 4, 1024], replicated, may hold values from -3 to 3
- var_embed: bfloat16 [48, 1024], replicated, may hold values from -6 to 6
- query: bfloat16 [1024], replicated, may hold values from -16 to 16
- key_weight: bfloat16 [1024, 1024], P('tok'), may hold values from -0.1875 to 0.1875
- value_weight: bfloat16 [1024, 1024], P('tok'), may hold values from -0.1875 to 0.1875
- out_weight: bfloat16 [1024, 1024], P('tok'), may hold values from -0.1875 to 0.1875
- cotangent: bfloat16 [4096, 1024], P(('tok', 'var')), may hold values from -6 to 6
Outputs:
- aggregated: bfloat16 [4096, 1024], P(('tok', 'var'))
- patch_grad: float32 [72, 4096], P('var', 'tok')
Inputs may be any that keep to these rules, and one draw needn't show every extreme that they name: `slot_var`: slot 9 * i + j belongs to index i of var. Every variable id stands in exactly one slot; empty slots hold -1. The live slots of an index come first and hold consecutive ids, rising from index to index. Every index holds at least one and at most 9 live slots, and some index holds exactly 9.
All inputs are finite; a program needn't handle non-finite values.
Results may differ from a plain program's by a relative error of at most 0.011.
Values may be sent and summed in bfloat16 or wider, within the bound.
No kernel may reach another device: no remote copies, remote signals or barrier semaphores. Data moves between devices by JAX's collectives and lax.ppermute only.
A program may use at most 128 MiB of HBM per device.

v0:
```python
import math
import jax
import jax.numpy as jnp
from jax import lax
from jax.sharding import PartitionSpec as P

H = 16
HD = 64
score_cap = 5.0
inv_sqrt_two = 1.0 / math.sqrt(2.0)
inv_sqrt_two_pi = 1.0 / math.sqrt(2.0 * math.pi)
f32 = jnp.float32
bf16 = jnp.bfloat16


def gelu_exact(inputs):
    return 0.5 * inputs * (1.0 + lax.erf(inputs * inv_sqrt_two))


def gelu_slope(inputs):
    return (
        0.5 * (1.0 + lax.erf(inputs * inv_sqrt_two))
        + inputs * jnp.exp(-0.5 * inputs * inputs) * inv_sqrt_two_pi
    )


def live_index(slot_var, var_total):
    ids = jnp.arange(var_total, dtype=jnp.int32)
    places = jnp.arange(slot_var.shape[0], dtype=jnp.int32)
    match = slot_var[None, :] == ids[:, None]
    return jnp.sum(jnp.where(match, places[None, :], 0), axis=1)


def split(x):
    hi = x.astype(bf16)
    lo = (x - hi.astype(f32)).astype(bf16)
    return (hi, lo)


def ein(spec, a, b):
    return jnp.einsum(spec, a, b, preferred_element_type=f32)


def ring_steps(block, n, perm_of):
    forward, backward = (block, block)
    behind, ahead = ([], [])
    for k in range(1, n // 2 + 1):
        forward = lax.ppermute(forward, "tok", perm_of(1))
        behind.append(forward)
        if k < n - k:
            backward = lax.ppermute(backward, "tok", perm_of(-1))
            ahead.append(backward)
    return jnp.stack([block] + behind + ahead[::-1])


def ring_gather(block, n_x, n_z):

    def along_z(step):
        return [(x * n_z + z, x * n_z + (z + step) % n_z) for x in range(n_x) for z in range(n_z)]

    def along_x(step):
        return [(x * n_z + z, (x + step) % n_x * n_z + z) for x in range(n_x) for z in range(n_z)]

    me = lax.axis_index("tok")
    my_z, my_x = (me % n_z, me // n_z)
    by_z = ring_steps(block, n_z, along_z)
    by_z = jnp.take(by_z, (my_z - jnp.arange(n_z)) % n_z, axis=0)
    by_x = ring_steps(by_z, n_x, along_x)
    by_x = jnp.take(by_x, (my_x - jnp.arange(n_x)) % n_x, axis=0)
    return by_x.reshape((n_x * n_z * block.shape[0],) + block.shape[1:])


def body(
    patches,
    slot_var,
    patch_weight,
    var_embed,
    query,
    key_weight,
    value_weight,
    out_weight,
    cotangent,
    *,
    n_var,
    n_tok,
    n_tok_x,
    n_tok_z
):
    var_total, pixels_per, width = patch_weight.shape
    local_slots = patches.shape[0]
    rows = key_weight.shape[0]
    tok_count = cotangent.shape[0]
    query_heads = query.reshape(H, HD).astype(f32)
    wq_rows = jnp.sum(key_weight.reshape(rows, H, HD).astype(f32) * query_heads[None], axis=2)
    wq_copies = jnp.broadcast_to(wq_rows[None], (n_tok, rows, H))
    wq_full = lax.all_to_all(wq_copies, "tok", 0, 0, tiled=True).reshape(n_tok * rows, H)
    wq_hi, wq_lo = split(wq_full)
    core = lax.axis_index("var") % 2
    mine = jnp.where(core == 0, value_weight, out_weight)
    gathered = ring_gather(mine, n_tok_x, n_tok_z)
    other = lax.ppermute(gathered, "var", [(i, i ^ 1) for i in range(n_var)])
    value_matrix = jnp.where(core == 0, gathered, other)
    out_matrix = jnp.where(core == 0, other, gathered)
    slot_pixels = lax.all_to_all(patches, "var", 2, 0, tiled=True)
    live_slot = live_index(slot_var, var_total)
    pixels = jnp.take(slot_pixels, live_slot, axis=0)
    pre_act = ein("vpt,vpd->vtd", pixels, patch_weight) + var_embed.astype(f32)[:, None, :]
    embedded = gelu_exact(pre_act).astype(bf16)
    slope = lax.optimization_barrier(gelu_slope(pre_act))
    raw_scores = (
        ein("vtd,dh->tvh", embedded, wq_hi) + ein("vtd,dh->tvh", embedded, wq_lo)
    ) / math.sqrt(HD)
    squashed = jnp.tanh(raw_scores / score_cap)
    exp_scores = jnp.exp(score_cap * squashed)
    attn_f32 = exp_scores / jnp.sum(exp_scores, axis=1, keepdims=True)
    attn_bf = attn_f32.astype(bf16)
    same_head = jnp.arange(H)[:, None] == jnp.arange(H)[None, :]
    mixed_in = ein("tvh,vtd->thd", attn_bf, embedded)
    mix_hi, mix_lo = split(mixed_in)
    rows_both = jnp.concatenate([mix_hi, mix_lo], axis=0).reshape(2 * tok_count * H, width)
    all_heads = jnp.dot(rows_both, value_matrix, preferred_element_type=f32).reshape(
        2, tok_count, H, H, HD
    )
    pooled = (
        jnp.sum(jnp.where(same_head[None, None, :, :, None], all_heads, 0.0), axis=(0, 3))
        .astype(bf16)
        .reshape(tok_count, width)
    )
    mixed_out = jnp.dot(pooled, out_matrix, preferred_element_type=f32).astype(bf16)
    cot_t = lax.optimization_barrier(cotangent.T)
    grad_pooled = (
        jnp.dot(out_matrix, cot_t, preferred_element_type=f32)
        .T.astype(bf16)
        .reshape(tok_count, H, HD)
    )
    by_head = jnp.where(
        same_head[:, None, None, :], grad_pooled.transpose(1, 2, 0)[:, :, :, None], 0
    )
    spread_t = jnp.dot(
        value_matrix, by_head.reshape(width, tok_count * H).astype(bf16), preferred_element_type=f32
    )
    spread = spread_t.reshape(width, tok_count, H).transpose(1, 2, 0)
    spread_hi, spread_lo = split(spread)
    both = ein("vtd,thd->tvh", embedded, jnp.concatenate([spread_hi, spread_lo], axis=1))
    grad_attn = both[:, :, :H] + both[:, :, H:]
    grad_scores = attn_f32 * (grad_attn - jnp.sum(attn_f32 * grad_attn, axis=1, keepdims=True))
    grad_raw = grad_scores * (1.0 - squashed * squashed) / math.sqrt(HD)
    raw_hi, raw_lo = split(grad_raw)
    left = jnp.concatenate([attn_bf, attn_bf, raw_hi, raw_hi, raw_lo], axis=2)
    wq_t = jnp.concatenate([wq_hi.T, wq_lo.T, wq_hi.T], axis=0)
    right = jnp.concatenate(
        [spread_hi, spread_lo, jnp.broadcast_to(wq_t[None], (tok_count,) + wq_t.shape)], axis=1
    )
    grad_embed = ein("tvk,tkd->vtd", left, right).astype(bf16)
    grad_pre = grad_embed.astype(f32) * slope
    partial = jnp.einsum(
        "vpt,vtd->vpd", pixels.astype(f32), grad_pre, precision=lax.Precision.HIGHEST
    ).reshape(var_total, pixels_per * width)
    slots = n_var * local_slots
    cols = partial.shape[1] // n_tok
    safe = jnp.clip(slot_var, 0, var_total - 1)
    slot_rows = jnp.where((slot_var >= 0)[:, None], jnp.take(partial, safe, axis=0), 0.0)
    blocks = slot_rows.reshape(n_var, local_slots, n_tok, cols)
    by_var = lax.all_to_all(blocks, "var", 0, 0, tiled=True).sum(axis=0)
    by_tok = lax.all_to_all(by_var.transpose(1, 0, 2), "tok", 0, 0, tiled=True).sum(axis=0)
    del slots
    return (mixed_out, by_tok)


def inner_ring(mesh, n_tok):
    try:
        row = mesh.devices[0]
        slow = [tuple(d.coords)[0] for d in row]
        size = next((i for i in range(1, n_tok) if slow[i] != slow[0]), n_tok)
        if n_tok % size == 0:
            return size
    except (AttributeError, TypeError, IndexError):
        pass
    return n_tok


def solution(mesh):
    import functools

    n_tok = mesh.shape["tok"]
    n_tok_z = inner_ring(mesh, n_tok)
    fn = functools.partial(
        body, n_var=mesh.shape["var"], n_tok=n_tok, n_tok_x=n_tok // n_tok_z, n_tok_z=n_tok_z
    )
    return jax.shard_map(
        fn,
        mesh=mesh,
        in_specs=(
            P("var", None, "tok"),
            P(),
            P(),
            P(),
            P(),
            P("tok", None),
            P("tok", None),
            P("tok", None),
            P(("tok", "var"), None),
        ),
        out_specs=(P(("tok", "var"), None), P("var", "tok")),
        check_vma=False,
    )
```

profile of v0, /device:TPU:32, one launch (start us, length us, event | category | flops | bytes accessed | tf_op | source)
XLA Modules:
  0.0 157.5 jit_solution(6378815027409704544)
XLA Ops:
  0.7 0.9 bitcast_dynamic-update-slice_fusion.7
  1.6 2.0 %collective-permute-start = (bf16[32,1024]{1,0:T(8,128)(2,1)S(1)}, bf16[32,1024]{1,0:T(8,128)(2,1)S(1)}, u32[]{:S(2)}, u32[]{:S(2)}) collective-permute-start(bf16[32,1024]{1,0:T(8,128)(2,1)S(1)} %get-tuple-element.9), channel_id=1, source_target_pairs={{0,1},{1,2},{2,3},{3,4},{4,5},{5,6},{6,7},{7,0},{8,9},{9,10},{10,1... | collective-permute-start | bytes 196616 | tf_op jit(solution)/shard_map/ppermute | solution.py:48
  3.7 0.9 copy.61
  5.3 4.5 %all-to-all-start.1 = ((bf16[8,2,288]{2,1,0:T(2,128)(2,1)}), bf16[8,2,288]{2,1,0:T(2,128)(2,1)S(1)}, u32[]{:S(2)}, u32[]{:S(2)}) async-start(bf16[8,2,288]{2,1,0:T(2,128)(2,1)} %reshape.267), calls=%async_computation.1 | async-start | bytes 24576 | tf_op jit(solution)/shard_map/all_to_all | solution.py:104
  10.6 1.0 reshape.227
  12.6 2.0 %collective-permute-start.1 = (bf16[32,1024]{1,0:T(8,128)(2,1)S(1)}, bf16[32,1024]{1,0:T(8,128)(2,1)S(1)}, u32[]{:S(2)}, u32[]{:S(2)}) collective-permute-start(bf16[32,1024]{1,0:T(8,128)(2,1)S(1)} %collective-permute-done), channel_id=1, source_target_pairs={{0,1},{1,2},{2,3},{3,4},{4,5},{5,6},{6,7},{7,0},{8,9},{9,10},{10,1... | collective-permute-start | bytes 196616 | tf_op jit(solution)/shard_map/ppermute | solution.py:48
  14.6 2.2 %collective-permute-start.5 = (bf16[32,1024]{1,0:T(8,128)(2,1)S(1)}, bf16[32,1024]{1,0:T(8,128)(2,1)S(1)}, u32[]{:S(2)}, u32[]{:S(2)}) collective-permute-start(bf16[32,1024]{1,0:T(8,128)(2,1)S(1)} %collective-permute-done.4), channel_id=1, source_target_pairs={{0,7},{1,0},{2,1},{3,2},{4,3},{5,4},{6,5},{7,6},{8,15},{9,8},{10,9... | collective-permute-start | bytes 196616 | tf_op jit(solution)/shard_map/ppermute | solution.py:51
  16.8 2.6 %collective-permute-done.1 = bf16[32,1024]{1,0:T(8,128)(2,1)S(1)} collective-permute-done((bf16[32,1024]{1,0:T(8,128)(2,1)S(1)}, bf16[32,1024]{1,0:T(8,128)(2,1)S(1)}, u32[]{:S(2)}, u32[]{:S(2)}) %collective-permute-start.1) | collective-permute-done | bytes 65568 | tf_op jit(solution)/shard_map/ppermute | solution.py:48
  20.2 2.3 %collective-permute-start.6 = (bf16[32,1024]{1,0:T(8,128)(2,1)S(1)}, bf16[32,1024]{1,0:T(8,128)(2,1)S(1)}, u32[]{:S(2)}, u32[]{:S(2)}) collective-permute-start(bf16[32,1024]{1,0:T(8,128)(2,1)S(1)} %collective-permute-done.5), channel_id=1, source_target_pairs={{0,7},{1,0},{2,1},{3,2},{4,3},{5,4},{6,5},{7,6},{8,15},{9,8},{10,9... | collective-permute-start | bytes 196616 | tf_op jit(solution)/shard_map/ppermute | solution.py:51
  22.5 2.1 %collective-permute-done.2 = bf16[32,1024]{1,0:T(8,128)(2,1)S(1)} collective-permute-done((bf16[32,1024]{1,0:T(8,128)(2,1)S(1)}, bf16[32,1024]{1,0:T(8,128)(2,1)S(1)}, u32[]{:S(2)}, u32[]{:S(2)}) %collective-permute-start.2) | collective-permute-done | bytes 65568 | tf_op jit(solution)/shard_map/ppermute | solution.py:48
  24.8 5.4 %collective-permute-done.3 = bf16[32,1024]{1,0:T(8,128)(2,1)S(1)} collective-permute-done((bf16[32,1024]{1,0:T(8,128)(2,1)S(1)}, bf16[32,1024]{1,0:T(8,128)(2,1)S(1)}, u32[]{:S(2)}, u32[]{:S(2)}) %collective-permute-start.3) | collective-permute-done | bytes 65568 | tf_op jit(solution)/shard_map/ppermute | solution.py:48
  30.9 1.6 collective-permute-start.7
  32.5 1.8 %collective-permute-start.9 = (bf16[8,32,1024]{2,1,0:T(8,128)(2,1)S(1)}, bf16[8,32,1024]{2,1,0:T(8,128)(2,1)S(1)}, u32[]{:S(2)}, u32[]{:S(2)}) collective-permute-start(bf16[8,32,1024]{2,1,0:T(8,128)(2,1)S(1)} %broadcast_select_fusion.6), channel_id=1, source_target_pairs={{0,24},{1,25},{2,26},{3,27},{4,28},{5,29},{6,30},{7,31},{8,0},{9,1... | collective-permute-start | bytes 1572872 | tf_op jit(solution)/shard_map/ppermute | solution.py:51
  34.3 9.3 %collective-permute-done.7 = bf16[8,32,1024]{2,1,0:T(8,128)(2,1)S(1)} collective-permute-done((bf16[8,32,1024]{2,1,0:T(8,128)(2,1)S(1)}, bf16[8,32,1024]{2,1,0:T(8,128)(2,1)S(1)}, u32[]{:S(2)}, u32[]{:S(2)}) %collective-permute-start.7) | collective-permute-done | bytes 524320 | tf_op jit(solution)/shard_map/ppermute | solution.py:48
  43.6 0.9 collective-permute-start.8
  44.9 10.5 %collective-permute-done.8 = bf16[8,32,1024]{2,1,0:T(8,128)(2,1)S(1)} collective-permute-done((bf16[8,32,1024]{2,1,0:T(8,128)(2,1)S(1)}, bf16[8,32,1024]{2,1,0:T(8,128)(2,1)S(1)}, u32[]{:S(2)}, u32[]{:S(2)}) %collective-permute-start.8) | collective-permute-done | bytes 524320 | tf_op jit(solution)/shard_map/ppermute | solution.py:48
  55.4 1.6 %pad_maximum_fusion = bf16[4,8,32,1024]{3,2,1,0:T(8,128)(2,1)} fusion(bf16[1,8,32,1024]{3,2,1,0:T(8,128)(2,1)S(1)} %bitcast.133, bf16[1,8,32,1024]{3,2,1,0:T(8,128)(2,1)S(1)} %bitcast.134, bf16[1,8,32,1024]{3,2,1,0:T(8,128)(2,1)S(1)} %bitcast.132, bf16[1,8,32,1024]{3,2,1,0:T(8,128)(2,1)S(1)} %bitcast_select_fusion.1), kind=kLoop, calls=%fused_computation.23 | loop fusion | flops 3145728 | bytes 4194304 | tf_op jit(solution)/shard_map/stack | solution.py:53
  57.0 2.3 %gather_fusion.2 = bf16[4,8,32,1024]{3,2,1,0:T(8,128)(2,1)S(1)} fusion(bf16[4,8,32,1024]{3,2,1,0:T(8,128)(2,1)} %pad_maximum_fusion, s32[1024]{0:T(1024)S(1)} %pad_clamp_fusion.1), kind=kCustom, calls=%fused_computation.2 | custom fusion | bytes 4194320 | tf_op jit(solution)/shard_map/jit(_take)/gather | solution.py:69
  59.3 1.8 %bitcast_select_fusion = bf16[1024,1024]{1,0:T(8,128)(2,1)} fusion(bf16[4,8,32,1024]{3,2,1,0:T(8,128)(2,1)S(1)} %gather_fusion.2, pred[1024]{0:T(1024)(128)(4,1)S(1)} %broadcast_in_dim.142), kind=kLoop, calls=%fused_computation.26 | loop fusion | flops 1048576 | bytes 4195328 | tf_op jit(solution)/shard_map/jit(_take)/select_n | solution.py:69
  63.8 9.5 %all-to-all-start = ((f32[32,1,512]{2,1,0:T(1,128)}), f32[32,1,512]{2,1,0:T(1,128)S(1)}, u32[]{:S(2)}, u32[]{:S(2)}) async-start(f32[32,1,512]{2,1,0:T(1,128)} %reshape.269), calls=%async_computation | async-start | bytes 131072 | tf_op jit(solution)/shard_map/all_to_all | solution.py:96
  74.7 3.8 %fusion.4 = (f32[48,16,1024]{2,1,0:T(8,128)}, bf16[48,16,1024]{2,1,0:T(8,128)(2,1)}) fusion(f32[48,1024]{1,0:T(8,128)S(1)} %convert_element_type.95, bf16[48,4,1024]{2,1,0:T(4,128)(2,1)S(1)} %copy-done, bf16[48,4,16]{2,1,0:T(4,128)(2,1)S(1)} %gather_fusion, pred[48]{0:T(512)(128)(4,1)S(1)} %compare_and_fusion.3), kind=kOutput, calls=%fused_computation.10 | convolution fusion | flops 15731712 | bytes 5314608 | tf_op jit(solution)/shard_map/vpt,vpd->vtd/dot_general | solution.py:41
  78.5 4.0 %all-to-all-done = f32[32,1,512]{2,1,0:T(1,128)S(1)} async-done(((f32[32,1,512]{2,1,0:T(1,128)}), f32[32,1,512]{2,1,0:T(1,128)S(1)}, u32[]{:S(2)}, u32[]{:S(2)}) %all-to-all-start) | async-done | bytes 65568 | tf_op jit(solution)/shard_map/all_to_all | solution.py:96
  83.0 0.8 reduce
  84.2 2.5 %fusion.30 = f32[16,48,16]{1,0,2:T(8,128)S(1)} fusion(bf16[48,16,1024]{2,1,0:T(8,128)(2,1)} %get-tuple-element.13, f32[1024,16]{0,1:T(8,128)S(1)} %reshape.224), kind=kOutput, calls=%fused_computation.52 | convolution fusion | flops 25182208 | bytes 1687552 | tf_op jit(solution)/shard_map/vtd,dh->tvh/dot_general | solution.py:41
  86.7 2.5 %bitcast_reduce_fusion = (f32[16,16]{1,0:T(8,128)S(1)}, f32[16,48,16]{1,0,2:T(8,128)S(1)}) fusion(f32[16,48,16]{1,0,2:T(8,128)S(1)} %fusion.30, bf16[48,16,1024]{2,1,0:T(8,128)(2,1)} %get-tuple-element.13, f32[1024,16]{0,1:T(8,128)S(1)} %reshape.224), kind=kOutput, calls=%fused_computation.60 | convolution fusion | flops 25280256 | bytes 1737728 | tf_op jit(solution)/shard_map/vtd,dh->tvh/dot_general | solution.py:41
  90.7 2.8 %subtract_convert_fusion.1 = (bf16[16,16,1024]{2,1,0:T(8,128)(2,1)}, bf16[16,16,1024]{2,1,0:T(8,128)(2,1)}) fusion(bf16[16,48,16]{1,2,0:T(8,128)(2,1)S(1)} %get-tuple-element.7, bf16[48,16,1024]{2,1,0:T(8,128)(2,1)S(1)} %copy-done.1), kind=kOutput, calls=%fused_computation.46 | convolution fusion | flops 26214400 | bytes 2646016 | tf_op jit(solution)/shard_map/tvh,vtd->thd/dot_general | solution.py:41
  93.5 2.2 %fusion.21 = bf16[16,1024]{1,0:T(8,128)(2,1)S(1)} fusion(bf16[1024,16]{0,1:T(8,128)(2,1)S(1)} %bitcast.137, bf16[1024,1024]{1,0:T(8,128)(2,1)} %collective-permute-done.10, bf16[1024,1024]{1,0:T(8,128)(2,1)} %bitcast_select_fusion, pred[]{:T(512)S(6)} %eq.58), kind=kOutput, calls=%fused_computation.39 | convolution fusion | flops 34619392 | bytes 4259841 | tf_op jit(solution)/shard_map/dot_general | solution.py:132
  96.5 1.0 broadcast_select_fusion.2
  97.5 1.5 select_n.196
  99.1 2.6 %subtract_convert_fusion = (bf16[16,16,1024]{2,1,0:T(8,128)(2,1)S(1)}, bf16[16,16,1024]{2,1,0:T(8,128)(2,1)S(1)}) fusion(bf16[16,16,1024]{2,1,0:T(8,128)(2,1)} %bitcast.128, bf16[1024,1024]{1,0:T(8,128)(2,1)} %bitcast_select_fusion, bf16[1024,1024]{1,0:T(8,128)(2,1)} %collective-permute-done.10, pred[]{:T(512)S(6)} %eq.58), kind=kOutput, calls=%fused_computation.45 | convolution fusion | flops 538968064 | bytes 5767169 | tf_op jit(solution)/shard_map/dot_general | solution.py:139
  101.7 1.1 fusion.22
  102.9 3.0 %constant_dynamic-update-slice_fusion.1 = (bf16[16,48,80]{1,2,0:T(8,128)(2,1)S(1)}, f32[16,48,16]{1,2,0:T(8,128)S(1)}) fusion(bf16[16,48,80]{1,2,0:T(8,128)(2,1)S(1)} %copy-done.14, f32[16,48,16]{1,0,2:T(8,128)S(1)} %copy-done.11, f32[16,48,32]{1,2,0:T(8,128)S(1)} %fusion.22, f32[16,16]{1,0:T(8,128)S(1)} %get-tuple-element.17), kind=kOutput, calls=%fused_computation.82 | output fusion | flops 172335 | bytes 999424 | tf_op jit(solution)/shard_map/sub | solution.py:146
  106.8 1.2 copy-done.3
  108.0 2.0 %fusion.5 = f32[48,4,1024]{2,1,0:T(4,128)S(1)} fusion(f32[48,16,1024]{2,1,0:T(8,128)S(1)} %copy-done.3, bf16[16,1024,48]{1,2,0:T(8,128)(2,1)S(1)} %fusion.7, bf16[48,4,16]{2,1,0:T(4,128)(2,1)S(1)} %copy-done.9, pred[48]{0:T(512)(128)(4,1)S(1)} %copy-done.18), kind=kOutput, calls=%fused_computation.12 | convolution fusion | flops 39324672 | bytes 5511216 | tf_op jit(solution)/shard_map/vpt,vtd->vpd/dot_general | solution.py:156
  110.5 2.1 %gather_fusion.3 = f32[72,4096]{1,0:T(8,128)} fusion(f32[48,4096]{1,0:T(8,128)S(1)} %bitcast.120, s32[1024]{0:T(1024)} %pad_clamp_fusion), kind=kCustom, calls=%fused_computation.3 | custom fusion | bytes 2359584 | tf_op jit(solution)/shard_map/jit(_take)/gather | solution.py:162
  112.5 1.5 copy.77
  114.1 1.3 select_select_fusion
  115.3 4.2 %all-to-all-start.2 = ((f32[8,9,32,128]{3,2,1,0:T(8,128)}), f32[8,9,32,128]{3,2,1,0:T(8,128)}, u32[]{:S(2)}, u32[]{:S(2)}) async-start(f32[8,9,32,128]{3,2,1,0:T(8,128)} %select_select_fusion), calls=%async_computation.2 | async-start | bytes 2359296 | tf_op jit(solution)/shard_map/all_to_all | solution.py:164
  119.6 1.1 pad_maximum_fusion.1
  120.7 1.8 %fusion.32 = bf16[1024,1024]{0,1:T(8,128)(2,1)} fusion(bf16[1024,1024]{1,0:T(8,128)(2,1)} %collective-permute-done.10, pred[]{:T(512)S(6)} %eq.58, bf16[4,8,32,1024]{3,2,1,0:T(8,128)(2,1)S(1)} %gather_fusion.2, pred[1024]{0:T(1024)(128)(4,1)S(1)} %broadcast_in_dim.142), kind=kLoop, calls=%fused_computation.54 | loop fusion | flops 2097152 | bytes 6292481 | tf_op jit(solution)/shard_map/dot_general | solution.py:121
  122.5 2.9 %copy.67 = bf16[1024,1024]{1,0:T(8,128)(2,1)S(1)} copy(bf16[1024,1024]{0,1:T(8,128)(2,1)} %fusion.32) | data formatting | bytes 4194304 | tf_op jit(solution)/shard_map/dot_general | solution.py:121
  125.4 3.2 %select_reduce_fusion = bf16[16,16,64]{2,1,0:T(8,128)(2,1)} fusion(pred[16,16]{0,1:T(8,128)(4,1)S(1)} %iota_compare_fusion.1, bf16[2,16,16,1024,1]{3,2,4,1,0:T(8,128)(2,1)S(1)} %bitcast.126, bf16[16,64,1024,1,1]{2,1,0,4,3:T(8,128)(2,1)S(1)} %bitcast.124), kind=kOutput, calls=%fused_computation.6 | convolution fusion | flops 1074774016 | bytes 3178752 | tf_op jit(solution)/shard_map/dot_general | solution.py:121
  128.6 1.0 convert_element_type.104
  129.6 7.3 %all-to-all-done.2 = f32[8,9,32,128]{3,2,1,0:T(8,128)} async-done(((f32[8,9,32,128]{3,2,1,0:T(8,128)}), f32[8,9,32,128]{3,2,1,0:T(8,128)}, u32[]{:S(2)}, u32[]{:S(2)}) %all-to-all-start.2) | async-done | bytes 1179680 | tf_op jit(solution)/shard_map/all_to_all | solution.py:164
  136.9 1.4 reduce_sum.71
  139.1 5.8 %all-to-all-start.3 = ((f32[32,9,128]{2,1,0:T(8,128)}), f32[32,9,128]{2,1,0:T(8,128)S(1)}, u32[]{:S(2)}, u32[]{:S(2)}) async-start(f32[32,9,128]{2,1,0:T(8,128)} %copy.71), calls=%async_computation.3 | async-start | bytes 524288 | tf_op jit(solution)/shard_map/all_to_all | solution.py:165
  144.9 2.6 %convolution_convert_fusion.1 = bf16[16,1024]{1,0:T(8,128)(2,1)} fusion(bf16[16,1024]{1,0:T(8,128)(2,1)S(1)} %convert_element_type.104, bf16[1024,1024]{1,0:T(8,128)(2,1)} %collective-permute-done.10, bf16[1024,1024]{1,0:T(8,128)(2,1)} %bitcast_select_fusion, pred[]{:T(512)S(6)} %eq.58), kind=kOutput, calls=%fused_computation.38 | convolution fusion | flops 34619392 | bytes 4259841 | tf_op jit(solution)/shard_map/dot_general | solution.py:129
  147.5 9.4 %all-to-all-done.3 = f32[32,9,128]{2,1,0:T(8,128)S(1)} async-done(((f32[32,9,128]{2,1,0:T(8,128)}), f32[32,9,128]{2,1,0:T(8,128)S(1)}, u32[]{:S(2)}, u32[]{:S(2)}) %all-to-all-start.3) | async-done | bytes 147488 | tf_op jit(solution)/shard_map/all_to_all | solution.py:165
  (106 shorter events, 14.5 us)
Async XLA Ops:
  0.6 74.1 %copy-start = (bf16[48,4,1024]{2,1,0:T(4,128)(2,1)S(1)}, bf16[48,4,1024]{2,1,0:T(4,128)(2,1)}, u32[]{:S(2)}) copy-start(bf16[48,4,1024]{2,1,0:T(4,128)(2,1)} %param.11) | copy-start | bytes 1179652
  0.7 31.8 %copy-start.19 = (s32[72]{0:T(128)S(1)}, s32[72]{0:T(128)}, u32[]{:S(2)}) copy-start(s32[72]{0:T(128)} %param.10) | copy-start | bytes 868
  1.6 11.0 %collective-permute-start = (bf16[32,1024]{1,0:T(8,128)(2,1)S(1)}, bf16[32,1024]{1,0:T(8,128)(2,1)S(1)}, u32[]{:S(2)}, u32[]{:S(2)}) collective-permute-start(bf16[32,1024]{1,0:T(8,128)(2,1)S(1)} %get-tuple-element.9), channel_id=1, source_target_pairs={{0,1},{1,2},{2,3},{3,4},{4,5},{5,6},{6,7},{7,0},{8,9},{9,10},{10,1... | collective-permute-start | bytes 196616 | tf_op jit(solution)/shard_map/ppermute | solution.py:48
  3.6 11.0 %collective-permute-start.4 = (bf16[32,1024]{1,0:T(8,128)(2,1)S(1)}, bf16[32,1024]{1,0:T(8,128)(2,1)S(1)}, u32[]{:S(2)}, u32[]{:S(2)}) collective-permute-start(bf16[32,1024]{1,0:T(8,128)(2,1)S(1)} %get-tuple-element.9), channel_id=1, source_target_pairs={{0,7},{1,0},{2,1},{3,2},{4,3},{5,4},{6,5},{7,6},{8,15},{9,8},{10,9... | collective-permute-start | bytes 196616 | tf_op jit(solution)/shard_map/ppermute | solution.py:51
  5.3 58.5 %all-to-all-start.1 = ((bf16[8,2,288]{2,1,0:T(2,128)(2,1)}), bf16[8,2,288]{2,1,0:T(2,128)(2,1)S(1)}, u32[]{:S(2)}, u32[]{:S(2)}) async-start(bf16[8,2,288]{2,1,0:T(2,128)(2,1)} %reshape.267), calls=%async_computation.1 | async-start | bytes 24576 | tf_op jit(solution)/shard_map/all_to_all | solution.py:104
  12.6 6.9 %collective-permute-start.1 = (bf16[32,1024]{1,0:T(8,128)(2,1)S(1)}, bf16[32,1024]{1,0:T(8,128)(2,1)S(1)}, u32[]{:S(2)}, u32[]{:S(2)}) collective-permute-start(bf16[32,1024]{1,0:T(8,128)(2,1)S(1)} %collective-permute-done), channel_id=1, source_target_pairs={{0,1},{1,2},{2,3},{3,4},{4,5},{5,6},{6,7},{7,0},{8,9},{9,10},{10,1... | collective-permute-start | bytes 196616 | tf_op jit(solution)/shard_map/ppermute | solution.py:48
  14.6 5.6 %collective-permute-start.5 = (bf16[32,1024]{1,0:T(8,128)(2,1)S(1)}, bf16[32,1024]{1,0:T(8,128)(2,1)S(1)}, u32[]{:S(2)}, u32[]{:S(2)}) collective-permute-start(bf16[32,1024]{1,0:T(8,128)(2,1)S(1)} %collective-permute-done.4), channel_id=1, source_target_pairs={{0,7},{1,0},{2,1},{3,2},{4,3},{5,4},{6,5},{7,6},{8,15},{9,8},{10,9... | collective-permute-start | bytes 196616 | tf_op jit(solution)/shard_map/ppermute | solution.py:51
  19.4 5.2 %collective-permute-start.2 = (bf16[32,1024]{1,0:T(8,128)(2,1)S(1)}, bf16[32,1024]{1,0:T(8,128)(2,1)S(1)}, u32[]{:S(2)}, u32[]{:S(2)}) collective-permute-start(bf16[32,1024]{1,0:T(8,128)(2,1)S(1)} %collective-permute-done.1), channel_id=1, source_target_pairs={{0,1},{1,2},{2,3},{3,4},{4,5},{5,6},{6,7},{7,0},{8,9},{9,10},{10,1... | collective-permute-start | bytes 196616 | tf_op jit(solution)/shard_map/ppermute | solution.py:48
  20.2 10.0 %collective-permute-start.6 = (bf16[32,1024]{1,0:T(8,128)(2,1)S(1)}, bf16[32,1024]{1,0:T(8,128)(2,1)S(1)}, u32[]{:S(2)}, u32[]{:S(2)}) collective-permute-start(bf16[32,1024]{1,0:T(8,128)(2,1)S(1)} %collective-permute-done.5), channel_id=1, source_target_pairs={{0,7},{1,0},{2,1},{3,2},{4,3},{5,4},{6,5},{7,6},{8,15},{9,8},{10,9... | collective-permute-start | bytes 196616 | tf_op jit(solution)/shard_map/ppermute | solution.py:51
  24.6 5.5 %collective-permute-start.3 = (bf16[32,1024]{1,0:T(8,128)(2,1)S(1)}, bf16[32,1024]{1,0:T(8,128)(2,1)S(1)}, u32[]{:S(2)}, u32[]{:S(2)}) collective-permute-start(bf16[32,1024]{1,0:T(8,128)(2,1)S(1)} %collective-permute-done.2), channel_id=1, source_target_pairs={{0,1},{1,2},{2,3},{3,4},{4,5},{5,6},{6,7},{7,0},{8,9},{9,10},{10,1... | collective-permute-start | bytes 196616 | tf_op jit(solution)/shard_map/ppermute | solution.py:48
  30.9 12.7 %collective-permute-start.7 = (bf16[8,32,1024]{2,1,0:T(8,128)(2,1)S(1)}, bf16[8,32,1024]{2,1,0:T(8,128)(2,1)S(1)}, u32[]{:S(2)}, u32[]{:S(2)}) collective-permute-start(bf16[8,32,1024]{2,1,0:T(8,128)(2,1)S(1)} %broadcast_select_fusion.6), channel_id=1, source_target_pairs={{0,8},{1,9},{2,10},{3,11},{4,12},{5,13},{6,14},{7,15},{8,16},{9,17... | collective-permute-start | bytes 1572872 | tf_op jit(solution)/shard_map/ppermute | solution.py:48
  32.5 42.2 %copy-start.17 = (pred[48]{0:T(512)(128)(4,1)}, pred[48]{0:T(512)(128)(4,1)S(1)}, u32[]{:S(2)}) copy-start(pred[48]{0:T(512)(128)(4,1)S(1)} %compare_and_fusion.3) | copy-start | bytes 148
  32.5 12.4 %collective-permute-start.9 = (bf16[8,32,1024]{2,1,0:T(8,128)(2,1)S(1)}, bf16[8,32,1024]{2,1,0:T(8,128)(2,1)S(1)}, u32[]{:S(2)}, u32[]{:S(2)}) collective-permute-start(bf16[8,32,1024]{2,1,0:T(8,128)(2,1)S(1)} %broadcast_select_fusion.6), channel_id=1, source_target_pairs={{0,24},{1,25},{2,26},{3,27},{4,28},{5,29},{6,30},{7,31},{8,0},{9,1... | collective-permute-start | bytes 1572872 | tf_op jit(solution)/shard_map/ppermute | solution.py:51
  43.6 11.8 %collective-permute-start.8 = (bf16[8,32,1024]{2,1,0:T(8,128)(2,1)S(1)}, bf16[8,32,1024]{2,1,0:T(8,128)(2,1)S(1)}, u32[]{:S(2)}, u32[]{:S(2)}) collective-permute-start(bf16[8,32,1024]{2,1,0:T(8,128)(2,1)S(1)} %collective-permute-done.7), channel_id=1, source_target_pairs={{0,8},{1,9},{2,10},{3,11},{4,12},{5,13},{6,14},{7,15},{8,16},{9,17... | collective-permute-start | bytes 1572872 | tf_op jit(solution)/shard_map/ppermute | solution.py:48
  59.3 2.4 %copy-start.12 = (bf16[48,1024]{1,0:T(8,128)(2,1)S(1)}, bf16[48,1024]{1,0:T(8,128)(2,1)}, u32[]{:S(2)}) copy-start(bf16[48,1024]{1,0:T(8,128)(2,1)} %param.12) | copy-start | bytes 294916
  61.1 32.4 %collective-permute-start.10 = (bf16[1024,1024]{1,0:T(8,128)(2,1)}, bf16[1024,1024]{1,0:T(8,128)(2,1)}, u32[]{:S(2)}, u32[]{:S(2)}) collective-permute-start(bf16[1024,1024]{1,0:T(8,128)(2,1)} %bitcast_select_fusion), channel_id=1, source_target_pairs={{0,32},{32,0},{64,96},{96,64},{128,160},{160,128},{192,224},{224,1... | collective-permute-start | bytes 6291464 | tf_op jit(solution)/shard_map/ppermute | solution.py:101
  63.8 18.7 %all-to-all-start = ((f32[32,1,512]{2,1,0:T(1,128)}), f32[32,1,512]{2,1,0:T(1,128)S(1)}, u32[]{:S(2)}, u32[]{:S(2)}) async-start(f32[32,1,512]{2,1,0:T(1,128)} %reshape.269), calls=%async_computation | async-start | bytes 131072 | tf_op jit(solution)/shard_map/all_to_all | solution.py:96
  74.7 3.8 %copy-start.8 = (bf16[48,4,16]{2,1,0:T(4,128)(2,1)}, bf16[48,4,16]{2,1,0:T(4,128)(2,1)S(1)}, u32[]{:S(2)}) copy-start(bf16[48,4,16]{2,1,0:T(4,128)(2,1)S(1)} %gather_fusion) | copy-start | bytes 18436
  84.2 6.6 %copy-start.1 = (bf16[48,16,1024]{2,1,0:T(8,128)(2,1)S(1)}, bf16[48,16,1024]{2,1,0:T(8,128)(2,1)}, u32[]{:S(2)}) copy-start(bf16[48,16,1024]{2,1,0:T(8,128)(2,1)} %get-tuple-element.13) | copy-start | bytes 4718596
  89.2 4.3 %copy-start.10 = (f32[16,48,16]{1,0,2:T(8,128)}, f32[16,48,16]{1,0,2:T(8,128)S(1)}, u32[]{:S(2)}) copy-start(f32[16,48,16]{1,0,2:T(8,128)S(1)} %get-tuple-element.18) | copy-start | bytes 147460
  89.2 4.3 %copy-start.20 = (bf16[16,1024]{1,0:T(8,128)(2,1)S(1)}, bf16[16,1024]{1,0:T(8,128)(2,1)}, u32[]{:S(2)}) copy-start(bf16[16,1024]{1,0:T(8,128)(2,1)} %param.17) | copy-start | bytes 98308
  89.4 0.7 copy-start.13
  99.1 2.6 %copy-start.2 = (bf16[48,16,1024]{2,1,0:T(8,128)(2,1)S(1)}, bf16[48,16,1024]{2,1,0:T(8,128)(2,1)}, u32[]{:S(2)}) copy-start(bf16[48,16,1024]{2,1,0:T(8,128)(2,1)} %get-tuple-element.13) | copy-start | bytes 4718596
  101.7 1.2 copy-start.11
  101.7 1.2 copy-start.14
  101.7 4.2 %copy-start.7 = (bf16[48,1024]{1,0:T(8,128)(2,1)S(1)}, bf16[48,1024]{1,0:T(8,128)(2,1)}, u32[]{:S(2)}) copy-start(bf16[48,1024]{1,0:T(8,128)(2,1)} %pad_maximum_fusion.2) | copy-start | bytes 294916
  106.1 1.9 %copy-start.3 = (f32[48,16,1024]{2,1,0:T(8,128)S(1)}, f32[48,16,1024]{2,1,0:T(8,128)}, u32[]{:S(2)}) copy-start(f32[48,16,1024]{2,1,0:T(8,128)} %get-tuple-element.12) | copy-start | bytes 9437188
  106.1 1.9 %copy-start.9 = (bf16[48,4,16]{2,1,0:T(4,128)(2,1)S(1)}, bf16[48,4,16]{2,1,0:T(4,128)(2,1)}, u32[]{:S(2)}) copy-start(bf16[48,4,16]{2,1,0:T(4,128)(2,1)} %copy-done.8) | copy-start | bytes 18436
  106.1 1.9 %copy-start.18 = (pred[48]{0:T(512)(128)(4,1)S(1)}, pred[48]{0:T(512)(128)(4,1)}, u32[]{:S(2)}) copy-start(pred[48]{0:T(512)(128)(4,1)} %copy-done.17) | copy-start | bytes 148
  112.5 1.5 copy-start.15
  112.5 1.5 copy-start.16
  114.0 5.5 %copy-start.4 = (bf16[16,16,1024]{2,1,0:T(8,128)(2,1)S(1)}, bf16[16,16,1024]{2,1,0:T(8,128)(2,1)}, u32[]{:S(2)}) copy-start(bf16[16,16,1024]{2,1,0:T(8,128)(2,1)} %get-tuple-element.10) | copy-start | bytes 1572868
  114.1 5.5 %copy-start.5 = (bf16[16,16,1024]{2,1,0:T(8,128)(2,1)S(1)}, bf16[16,16,1024]{2,1,0:T(8,128)(2,1)}, u32[]{:S(2)}) copy-start(bf16[16,16,1024]{2,1,0:T(8,128)(2,1)} %get-tuple-element.11) | copy-start | bytes 1572868
  115.3 21.6 %all-to-all-start.2 = ((f32[8,9,32,128]{3,2,1,0:T(8,128)}), f32[8,9,32,128]{3,2,1,0:T(8,128)}, u32[]{:S(2)}, u32[]{:S(2)}) async-start(f32[8,9,32,128]{3,2,1,0:T(8,128)} %select_select_fusion), calls=%async_computation.2 | async-start | bytes 2359296 | tf_op jit(solution)/shard_map/all_to_all | solution.py:164
  122.5 3.0 %copy-start.6 = (bf16[32,16,1024]{2,1,0:T(8,128)(2,1)S(1)}, bf16[32,16,1024]{2,1,0:T(8,128)(2,1)}, u32[]{:S(2)}) copy-start(bf16[32,16,1024]{2,1,0:T(8,128)(2,1)} %pad_maximum_fusion.1) | copy-start | bytes 3145732
  139.1 17.8 %all-to-all-start.3 = ((f32[32,9,128]{2,1,0:T(8,128)}), f32[32,9,128]{2,1,0:T(8,128)S(1)}, u32[]{:S(2)}, u32[]{:S(2)}) async-start(f32[32,9,128]{2,1,0:T(8,128)} %copy.71), calls=%async_computation.3 | async-start | bytes 524288 | tf_op jit(solution)/shard_map/all_to_all | solution.py:165
where the time goes:
time: 158 us
  waiting for transfers between devices  51.2 us (32%)
  starting transfers between devices  37.3 us (24%)
  matrix products  26 us (16%)
  local copies, waits for them, and re-layouts  24 us (15%)
  other arithmetic  17.8 us (11%)
    ppermute x6, waiting for transfers between devices, ring_steps(): forward = lax.ppermute(forward, 'tok', perm_of(1))  29.9 us
    dot_general x6, matrix products, ein(): return jnp.einsum(spec, a, b, preferred_element_type=f32)  13.3 us
    all_to_all x1, starting transfers between devices, body(): lax.all_to_all(wq_copies, 'tok', 0, 0, tiled=True).reshape(n_tok * rows, H)  9.54 us
    all_to_all x1, waiting for transfers between devices, body(): lax.all_to_all(by_var.transpose(1, 0, 2), 'tok', 0, 0, tiled=True)  9.36 us
    all_to_all x1, waiting for transfers between devices, body(): by_var = lax.all_to_all(blocks, 'var', 0, 0, tiled=True).sum(axis=0)  7.33 us
    unnamed x57, local copies, waits for them, and re-layouts  6.9 us
    ppermute x6, starting transfers between devices, ring_steps(): forward = lax.ppermute(forward, 'tok', perm_of(1))  6.75 us
    ppermute x4, starting transfers between devices, ring_steps(): backward = lax.ppermute(backward, 'tok', perm_of(-1))  6.48 us
  transfers between devices with their start and end apart: 15, of which 9 were waited for; matrix products, arithmetic and copies ran while one was open for 26% of the time, Pallas kernels for 0%

commit v1 on v0

--- a/solution.py
+++ b/solution.py
@@ -101,7 +101,25 @@
     other = lax.ppermute(gathered, "var", [(i, i ^ 1) for i in range(n_var)])
     value_matrix = jnp.where(core == 0, gathered, other)
     out_matrix = jnp.where(core == 0, other, gathered)
-    slot_pixels = lax.all_to_all(patches, "var", 2, 0, tiled=True)
+    row_out = lax.axis_size("var")
+    base_arr, long_array = (row_out, lax.axis_index("var"))
+    current_block = list(patches.shape)
+    piece_now = patches.shape[2] // base_arr
+    current_block[2] = piece_now
+    state_now = current_block[0]
+    current_block[0] = state_now * base_arr
+    slot_pixels = jnp.zeros(current_block, patches.dtype)
+    for nth in tuple(range(base_arr)):
+        frame_out = lax.dynamic_slice_in_dim(
+            patches, (long_array ^ nth) * piece_now, piece_now, axis=2
+        )
+        if nth:
+            frame_out = lax.ppermute(
+                frame_out, "var", [(tick, tick ^ nth) for tick in range(base_arr)]
+            )
+        slot_pixels = lax.dynamic_update_slice_in_dim(
+            slot_pixels, frame_out, (long_array ^ nth) * state_now, axis=0
+        )
     live_slot = live_index(slot_var, var_total)
     pixels = jnp.take(slot_pixels, live_slot, axis=0)
     pre_act = ein("vpt,vpd->vtd", pixels, patch_weight) + var_embed.astype(f32)[:, None, :]

time: 158 us -> 157 us (level)
  waiting for transfers between devices: 51.2 us -> 39.1 us
  starting transfers between devices: 37.3 us -> 48.5 us
    ppermute x6, waiting for transfers between devices: 29.9 us -> 11.3 us  [ring_steps(): forward = lax.ppermute(forward, 'tok', perm_of(1))]
    ppermute x4, waiting for transfers between devices: 0.55 us -> 11.1 us  [ring_steps(): backward = lax.ppermute(backward, 'tok', perm_of(-1))]
    ppermute x0 -> x7, starting transfers between devices: none -> 8.41 us  [body(): lax.ppermute(frame_out, 'var', [(tick, tick ^ nth) for tick in range(base...]
    all_to_all x1 -> x0, starting transfers between devices: 4.47 us -> none  [body(): slot_pixels = lax.all_to_all(patches, 'var', 2, 0, tiled=True)]
    all_to_all x1, waiting for transfers between devices: 4 us -> 0.01 us  [body(): lax.all_to_all(wq_copies, 'tok', 0, 0, tiled=True).reshape(n_tok * rows, H)]
    all_to_all x1, starting transfers between devices: 5.78 us -> 9.39 us  [body(): lax.all_to_all(by_var.transpose(1, 0, 2), 'tok', 0, 0, tiled=True)]
    all_to_all x1, starting transfers between devices: 9.54 us -> 12.4 us  [body(): lax.all_to_all(wq_copies, 'tok', 0, 0, tiled=True).reshape(n_tok * rows, H)]
    unnamed x57 -> x52, local copies, waits for them, and re-layouts: 6.9 us -> 4.93 us
  transfers between devices with their start and end apart: 15 -> 21, of which waited for: 9 -> 9; matrix products, arithmetic and copies ran while one was open for 26% -> 26% of each run, Pallas kernels for 0% -> 0%
where the time goes in v1:
time: 157 us; the launch traced here: 156 us
  starting transfers between devices  48.5 us (31%)
  waiting for transfers between devices  39.1 us (25%)
  matrix products  26.1 us (17%)
  local copies, waits for them, and re-layouts  23 us (15%)
  other arithmetic  18.5 us (12%)
    dot_general x6, matrix products, ein(): return jnp.einsum(spec, a, b, preferred_element_type=f32)  13.4 us
    all_to_all x1, starting transfers between devices, body(): lax.all_to_all(wq_copies, 'tok', 0, 0, tiled=True).reshape(n_tok * rows, H)  12.4 us
    ppermute x6, waiting for transfers between devices, ring_steps(): forward = lax.ppermute(forward, 'tok', perm_of(1))  11.3 us
    ppermute x4, waiting for transfers between devices, ring_steps(): backward = lax.ppermute(backward, 'tok', perm_of(-1))  11.1 us
    all_to_all x1, starting transfers between devices, body(): lax.all_to_all(by_var.transpose(1, 0, 2), 'tok', 0, 0, tiled=True)  9.39 us
    all_to_all x1, waiting for transfers between devices, body(): lax.all_to_all(by_var.transpose(1, 0, 2), 'tok', 0, 0, tiled=True)  9.36 us
    ppermute x6, starting transfers between devices, ring_steps(): forward = lax.ppermute(forward, 'tok', perm_of(1))  8.58 us
    ppermute x7, starting transfers between devices, body(): lax.ppermute(frame_out, 'var', [(tick, tick ^ nth) for tick in range(base...  8.41 us
  transfers between devices with their start and end apart: 21, of which 9 were waited for; matrix products, arithmetic and copies ran while one was open for 26% of the time, Pallas kernels for 0%

profile of v1, /device:TPU:32, one launch (start us, length us, event | category | flops | bytes accessed | tf_op | source)
XLA Modules:
  0.0 156.5 jit_solution(5017771163051278418)
XLA Ops:
  1.6 2.0 %collective-permute-start.7 = (bf16[32,1024]{1,0:T(8,128)(2,1)S(1)}, bf16[32,1024]{1,0:T(8,128)(2,1)S(1)}, u32[]{:S(2)}, u32[]{:S(2)}) collective-permute-start(bf16[32,1024]{1,0:T(8,128)(2,1)S(1)} %get-tuple-element.9), channel_id=1, source_target_pairs={{0,1},{1,2},{2,3},{3,4},{4,5},{5,6},{6,7},{7,0},{8,9},{9,10},{10,1... | collective-permute-start | bytes 196616 | tf_op jit(solution)/shard_map/ppermute | solution.py:48
  3.7 1.1 constant_dynamic-slice_fusion
  4.9 1.7 %collective-permute-start.1 = (bf16[9,4,16]{2,1,0:T(4,128)(2,1)S(1)}, bf16[9,4,16]{2,1,0:T(4,128)(2,1)S(1)}, u32[]{:S(2)}, u32[]{:S(2)}) collective-permute-start(bf16[9,4,16]{2,1,0:T(4,128)(2,1)S(1)} %get-tuple-element.20), channel_id=1, source_target_pairs={{0,64},{32,96},{64,0},{96,32},{128,192},{160,224},{192,128},{224,1... | collective-permute-start | bytes 3464 | tf_op jit(solution)/shard_map/ppermute | solution.py:117
  6.8 1.0 reshape.227
  9.6 12.4 %all-to-all-start = ((f32[32,1,512]{2,1,0:T(1,128)}), f32[32,1,512]{2,1,0:T(1,128)S(1)}, u32[]{:S(2)}, u32[]{:S(2)}) async-start(f32[32,1,512]{2,1,0:T(1,128)} %reshape.267), calls=%async_computation | async-start | bytes 131072 | tf_op jit(solution)/shard_map/all_to_all | solution.py:96
  24.2 1.5 collective-permute-start.8
  26.4 2.1 %collective-permute-done.8 = bf16[32,1024]{1,0:T(8,128)(2,1)S(1)} collective-permute-done((bf16[32,1024]{1,0:T(8,128)(2,1)S(1)}, bf16[32,1024]{1,0:T(8,128)(2,1)S(1)}, u32[]{:S(2)}, u32[]{:S(2)}) %collective-permute-start.8) | collective-permute-done | bytes 65568 | tf_op jit(solution)/shard_map/ppermute | solution.py:48
  28.6 1.5 collective-permute-start.9
  30.0 2.8 %collective-permute-done.9 = bf16[32,1024]{1,0:T(8,128)(2,1)S(1)} collective-permute-done((bf16[32,1024]{1,0:T(8,128)(2,1)S(1)}, bf16[32,1024]{1,0:T(8,128)(2,1)S(1)}, u32[]{:S(2)}, u32[]{:S(2)}) %collective-permute-start.9) | collective-permute-done | bytes 65568 | tf_op jit(solution)/shard_map/ppermute | solution.py:48
  32.8 1.5 collective-permute-start.10
  34.3 3.3 %collective-permute-start.3 = (bf16[9,4,16]{2,1,0:T(4,128)(2,1)S(1)}, bf16[9,4,16]{2,1,0:T(4,128)(2,1)S(1)}, u32[]{:S(2)}, u32[]{:S(2)}) collective-permute-start(bf16[9,4,16]{2,1,0:T(4,128)(2,1)S(1)} %get-tuple-element.18), channel_id=1, source_target_pairs={{0,128},{32,160},{64,192},{96,224},{128,0},{160,32},{192,64},{224,... | collective-permute-start | bytes 3464 | tf_op jit(solution)/shard_map/ppermute | solution.py:117
  37.8 3.2 %collective-permute-start.13 = (bf16[32,1024]{1,0:T(8,128)(2,1)S(1)}, bf16[32,1024]{1,0:T(8,128)(2,1)S(1)}, u32[]{:S(2)}, u32[]{:S(2)}) collective-permute-start(bf16[32,1024]{1,0:T(8,128)(2,1)S(1)} %collective-permute-done.12), channel_id=1, source_target_pairs={{0,7},{1,0},{2,1},{3,2},{4,3},{5,4},{6,5},{7,6},{8,15},{9,8},{10,9... | collective-permute-start | bytes 196616 | tf_op jit(solution)/shard_map/ppermute | solution.py:51
  41.1 1.9 %collective-permute-done.13 = bf16[32,1024]{1,0:T(8,128)(2,1)S(1)} collective-permute-done((bf16[32,1024]{1,0:T(8,128)(2,1)S(1)}, bf16[32,1024]{1,0:T(8,128)(2,1)S(1)}, u32[]{:S(2)}, u32[]{:S(2)}) %collective-permute-start.13) | collective-permute-done | bytes 65568 | tf_op jit(solution)/shard_map/ppermute | solution.py:51
  43.7 1.9 %collective-permute-start.14 = (bf16[8,32,1024]{2,1,0:T(8,128)(2,1)S(1)}, bf16[8,32,1024]{2,1,0:T(8,128)(2,1)S(1)}, u32[]{:S(2)}, u32[]{:S(2)}) collective-permute-start(bf16[8,32,1024]{2,1,0:T(8,128)(2,1)S(1)} %broadcast_select_fusion.6), channel_id=1, source_target_pairs={{0,8},{1,9},{2,10},{3,11},{4,12},{5,13},{6,14},{7,15},{8,16},{9,17... | collective-permute-start | bytes 1572872 | tf_op jit(solution)/shard_map/ppermute | solution.py:48
  47.2 3.1 %collective-permute-start.5 = (bf16[9,4,16]{2,1,0:T(4,128)(2,1)S(1)}, bf16[9,4,16]{2,1,0:T(4,128)(2,1)S(1)}, u32[]{:S(2)}, u32[]{:S(2)}) collective-permute-start(bf16[9,4,16]{2,1,0:T(4,128)(2,1)S(1)} %get-tuple-element.23), channel_id=1, source_target_pairs={{0,192},{32,224},{64,128},{96,160},{128,64},{160,96},{192,0},{224,... | collective-permute-start | bytes 3464 | tf_op jit(solution)/shard_map/ppermute | solution.py:117
  50.3 1.5 collective-permute-start.16
  51.8 3.5 %collective-permute-done.14 = bf16[8,32,1024]{2,1,0:T(8,128)(2,1)S(1)} collective-permute-done((bf16[8,32,1024]{2,1,0:T(8,128)(2,1)S(1)}, bf16[8,32,1024]{2,1,0:T(8,128)(2,1)S(1)}, u32[]{:S(2)}, u32[]{:S(2)}) %collective-permute-start.14) | collective-permute-done | bytes 524320 | tf_op jit(solution)/shard_map/ppermute | solution.py:48
  55.9 9.1 %collective-permute-done.16 = bf16[8,32,1024]{2,1,0:T(8,128)(2,1)S(1)} collective-permute-done((bf16[8,32,1024]{2,1,0:T(8,128)(2,1)S(1)}, bf16[8,32,1024]{2,1,0:T(8,128)(2,1)S(1)}, u32[]{:S(2)}, u32[]{:S(2)}) %collective-permute-start.16) | collective-permute-done | bytes 524320 | tf_op jit(solution)/shard_map/ppermute | solution.py:51
  65.1 2.6 %collective-permute-done.15 = bf16[8,32,1024]{2,1,0:T(8,128)(2,1)S(1)} collective-permute-done((bf16[8,32,1024]{2,1,0:T(8,128)(2,1)S(1)}, bf16[8,32,1024]{2,1,0:T(8,128)(2,1)S(1)}, u32[]{:S(2)}, u32[]{:S(2)}) %collective-permute-start.15) | collective-permute-done | bytes 524320 | tf_op jit(solution)/shard_map/ppermute | solution.py:48
  67.7 1.6 %pad_maximum_fusion = bf16[4,8,32,1024]{3,2,1,0:T(8,128)(2,1)} fusion(bf16[1,8,32,1024]{3,2,1,0:T(8,128)(2,1)S(1)} %bitcast.123, bf16[1,8,32,1024]{3,2,1,0:T(8,128)(2,1)S(1)} %bitcast.124, bf16[1,8,32,1024]{3,2,1,0:T(8,128)(2,1)S(1)} %bitcast.122, bf16[1,8,32,1024]{3,2,1,0:T(8,128)(2,1)S(1)} %bitcast_select_fusion.1), kind=kLoop, calls=%fused_computation.23 | loop fusion | flops 3145728 | bytes 4194304 | tf_op jit(solution)/shard_map/stack | solution.py:53
  69.3 2.3 %gather_fusion.2 = bf16[4,8,32,1024]{3,2,1,0:T(8,128)(2,1)S(1)} fusion(bf16[4,8,32,1024]{3,2,1,0:T(8,128)(2,1)} %pad_maximum_fusion, s32[1024]{0:T(1024)S(1)} %pad_clamp_fusion.1), kind=kCustom, calls=%fused_computation.2 | custom fusion | bytes 4194320 | tf_op jit(solution)/shard_map/jit(_take)/gather | solution.py:69
  71.5 1.7 %bitcast_select_fusion = bf16[1024,1024]{1,0:T(8,128)(2,1)} fusion(bf16[4,8,32,1024]{3,2,1,0:T(8,128)(2,1)S(1)} %gather_fusion.2, pred[1024]{0:T(1024)(128)(4,1)S(1)} %broadcast_in_dim.146), kind=kLoop, calls=%fused_computation.26 | loop fusion | flops 1048576 | bytes 4195328 | tf_op jit(solution)/shard_map/jit(_take)/select_n | solution.py:69
  74.0 3.8 %fusion.4 = (f32[48,16,1024]{2,1,0:T(8,128)}, bf16[48,16,1024]{2,1,0:T(8,128)(2,1)}) fusion(f32[48,1024]{1,0:T(8,128)S(1)} %convert_element_type.95, bf16[48,4,1024]{2,1,0:T(4,128)(2,1)S(1)} %copy-done, bf16[48,4,16]{2,1,0:T(4,128)(2,1)S(1)} %gather_fusion, pred[48]{0:T(512)(128)(4,1)S(1)} %compare_and_fusion.3), kind=kOutput, calls=%fused_computation.10 | convolution fusion | flops 15731712 | bytes 5314608 | tf_op jit(solution)/shard_map/vpt,vpd->vtd/dot_general | solution.py:41
  79.5 2.5 %fusion.30 = f32[16,48,16]{1,0,2:T(8,128)S(1)} fusion(bf16[48,16,1024]{2,1,0:T(8,128)(2,1)} %get-tuple-element.13, f32[1024,16]{0,1:T(8,128)S(1)} %reshape.224), kind=kOutput, calls=%fused_computation.52 | convolution fusion | flops 25182208 | bytes 1687552 | tf_op jit(solution)/shard_map/vtd,dh->tvh/dot_general | solution.py:41
  82.0 2.5 %bitcast_reduce_fusion = (f32[16,16]{1,0:T(8,128)S(1)}, f32[16,48,16]{1,0,2:T(8,128)S(1)}) fusion(f32[16,48,16]{1,0,2:T(8,128)S(1)} %fusion.30, bf16[48,16,1024]{2,1,0:T(8,128)(2,1)} %get-tuple-element.13, f32[1024,16]{0,1:T(8,128)S(1)} %reshape.224), kind=kOutput, calls=%fused_computation.60 | convolution fusion | flops 25280256 | bytes 1737728 | tf_op jit(solution)/shard_map/vtd,dh->tvh/dot_general | solution.py:41
  86.1 2.7 %subtract_convert_fusion.1 = (bf16[16,16,1024]{2,1,0:T(8,128)(2,1)}, bf16[16,16,1024]{2,1,0:T(8,128)(2,1)}) fusion(bf16[16,48,16]{1,2,0:T(8,128)(2,1)S(1)} %get-tuple-element.7, bf16[48,16,1024]{2,1,0:T(8,128)(2,1)S(1)} %copy-done.1), kind=kOutput, calls=%fused_computation.46 | convolution fusion | flops 26214400 | bytes 2646016 | tf_op jit(solution)/shard_map/tvh,vtd->thd/dot_general | solution.py:41
  88.9 2.2 %fusion.21 = bf16[16,1024]{1,0:T(8,128)(2,1)S(1)} fusion(bf16[1024,16]{0,1:T(8,128)(2,1)S(1)} %bitcast.126, bf16[1024,1024]{1,0:T(8,128)(2,1)} %collective-permute-done.17, bf16[1024,1024]{1,0:T(8,128)(2,1)} %bitcast_select_fusion, pred[]{:T(512)S(6)} %eq.58), kind=kOutput, calls=%fused_computation.39 | convolution fusion | flops 34619392 | bytes 4259841 | tf_op jit(solution)/shard_map/dot_general | solution.py:150
  91.9 1.0 broadcast_select_fusion.2
  92.9 1.5 select_n.260
  94.4 2.6 %subtract_convert_fusion = (bf16[16,16,1024]{2,1,0:T(8,128)(2,1)S(1)}, bf16[16,16,1024]{2,1,0:T(8,128)(2,1)S(1)}) fusion(bf16[16,16,1024]{2,1,0:T(8,128)(2,1)} %bitcast.121, bf16[1024,1024]{1,0:T(8,128)(2,1)} %bitcast_select_fusion, bf16[1024,1024]{1,0:T(8,128)(2,1)} %collective-permute-done.17, pred[]{:T(512)S(6)} %eq.58), kind=kOutput, calls=%fused_computation.45 | convolution fusion | flops 538968064 | bytes 5767169 | tf_op jit(solution)/shard_map/dot_general | solution.py:157
  97.1 1.1 fusion.22
  98.2 3.0 %constant_dynamic-update-slice_fusion.1 = (bf16[16,48,80]{1,2,0:T(8,128)(2,1)S(1)}, f32[16,48,16]{1,2,0:T(8,128)S(1)}) fusion(bf16[16,48,80]{1,2,0:T(8,128)(2,1)S(1)} %copy-done.14, f32[16,48,16]{1,0,2:T(8,128)S(1)} %copy-done.11, f32[16,48,32]{1,2,0:T(8,128)S(1)} %fusion.22, f32[16,16]{1,0:T(8,128)S(1)} %get-tuple-element.25), kind=kOutput, calls=%fused_computation.81 | output fusion | flops 172335 | bytes 999424 | tf_op jit(solution)/shard_map/sub | solution.py:164
  102.1 1.2 copy-done.3
  103.3 2.0 %fusion.5 = f32[48,4,1024]{2,1,0:T(4,128)S(1)} fusion(f32[48,16,1024]{2,1,0:T(8,128)S(1)} %copy-done.3, bf16[16,1024,48]{1,2,0:T(8,128)(2,1)S(1)} %fusion.7, bf16[48,4,16]{2,1,0:T(4,128)(2,1)S(1)} %copy-done.9, pred[48]{0:T(512)(128)(4,1)S(1)} %copy-done.18), kind=kOutput, calls=%fused_computation.12 | convolution fusion | flops 39324672 | bytes 5511216 | tf_op jit(solution)/shard_map/vpt,vtd->vpd/dot_general | solution.py:174
  105.8 2.1 %gather_fusion.3 = f32[72,4096]{1,0:T(8,128)} fusion(f32[48,4096]{1,0:T(8,128)S(1)} %bitcast.113, s32[1024]{0:T(1024)} %pad_clamp_fusion), kind=kCustom, calls=%fused_computation.3 | custom fusion | bytes 2359584 | tf_op jit(solution)/shard_map/jit(_take)/gather | solution.py:180
  107.9 1.5 copy.62
  109.4 1.3 select_select_fusion
  110.7 4.2 %all-to-all-start.1 = ((f32[8,9,32,128]{3,2,1,0:T(8,128)}), f32[8,9,32,128]{3,2,1,0:T(8,128)}, u32[]{:S(2)}, u32[]{:S(2)}) async-start(f32[8,9,32,128]{3,2,1,0:T(8,128)} %select_select_fusion), calls=%async_computation.1 | async-start | bytes 2359296 | tf_op jit(solution)/shard_map/all_to_all | solution.py:182
  114.9 1.1 pad_maximum_fusion.1
  116.0 1.8 %fusion.32 = bf16[1024,1024]{0,1:T(8,128)(2,1)} fusion(bf16[1024,1024]{1,0:T(8,128)(2,1)} %collective-permute-done.17, pred[]{:T(512)S(6)} %eq.58, bf16[4,8,32,1024]{3,2,1,0:T(8,128)(2,1)S(1)} %gather_fusion.2, pred[1024]{0:T(1024)(128)(4,1)S(1)} %broadcast_in_dim.146), kind=kLoop, calls=%fused_computation.54 | loop fusion | flops 2097152 | bytes 6292481 | tf_op jit(solution)/shard_map/dot_general | solution.py:139
  117.8 2.9 %copy.53 = bf16[1024,1024]{1,0:T(8,128)(2,1)S(1)} copy(bf16[1024,1024]{0,1:T(8,128)(2,1)} %fusion.32) | data formatting | bytes 4194304 | tf_op jit(solution)/shard_map/dot_general | solution.py:139
  120.8 3.2 %select_reduce_fusion = bf16[16,16,64]{2,1,0:T(8,128)(2,1)} fusion(pred[16,16]{0,1:T(8,128)(4,1)S(1)} %iota_compare_fusion.1, bf16[2,16,16,1024,1]{3,2,4,1,0:T(8,128)(2,1)S(1)} %bitcast.119, bf16[16,64,1024,1,1]{2,1,0,4,3:T(8,128)(2,1)S(1)} %bitcast.117), kind=kOutput, calls=%fused_computation.6 | convolution fusion | flops 1074774016 | bytes 3178752 | tf_op jit(solution)/shard_map/dot_general | solution.py:139
  124.0 1.0 convert_element_type.104
  125.0 7.3 %all-to-all-done.1 = f32[8,9,32,128]{3,2,1,0:T(8,128)} async-done(((f32[8,9,32,128]{3,2,1,0:T(8,128)}), f32[8,9,32,128]{3,2,1,0:T(8,128)}, u32[]{:S(2)}, u32[]{:S(2)}) %all-to-all-start.1) | async-done | bytes 1179680 | tf_op jit(solution)/shard_map/all_to_all | solution.py:182
  132.3 1.4 reduce_sum.71
  134.4 9.4 %all-to-all-start.2 = ((f32[32,9,128]{2,1,0:T(8,128)}), f32[32,9,128]{2,1,0:T(8,128)S(1)}, u32[]{:S(2)}, u32[]{:S(2)}) async-start(f32[32,9,128]{2,1,0:T(8,128)} %copy.57), calls=%async_computation.2 | async-start | bytes 524288 | tf_op jit(solution)/shard_map/all_to_all | solution.py:183
  143.8 2.6 %convolution_convert_fusion.1 = bf16[16,1024]{1,0:T(8,128)(2,1)} fusion(bf16[16,1024]{1,0:T(8,128)(2,1)S(1)} %convert_element_type.104, bf16[1024,1024]{1,0:T(8,128)(2,1)} %collective-permute-done.17, bf16[1024,1024]{1,0:T(8,128)(2,1)} %bitcast_select_fusion, pred[]{:T(512)S(6)} %eq.58), kind=kOutput, calls=%fused_computation.38 | convolution fusion | flops 34619392 | bytes 4259841 | tf_op jit(solution)/shard_map/dot_general | solution.py:147
  146.5 9.4 %all-to-all-done.2 = f32[32,9,128]{2,1,0:T(8,128)S(1)} async-done(((f32[32,9,128]{2,1,0:T(8,128)}), f32[32,9,128]{2,1,0:T(8,128)S(1)}, u32[]{:S(2)}, u32[]{:S(2)}) %all-to-all-start.2) | async-done | bytes 147488 | tf_op jit(solution)/shard_map/all_to_all | solution.py:183
  (120 shorter events, 16.3 us)
Async XLA Ops:
  0.6 73.3 %copy-start = (bf16[48,4,1024]{2,1,0:T(4,128)(2,1)S(1)}, bf16[48,4,1024]{2,1,0:T(4,128)(2,1)}, u32[]{:S(2)}) copy-start(bf16[48,4,1024]{2,1,0:T(4,128)(2,1)} %param.11) | copy-start | bytes 1179652
  1.6 22.6 %collective-permute-start.7 = (bf16[32,1024]{1,0:T(8,128)(2,1)S(1)}, bf16[32,1024]{1,0:T(8,128)(2,1)S(1)}, u32[]{:S(2)}, u32[]{:S(2)}) collective-permute-start(bf16[32,1024]{1,0:T(8,128)(2,1)S(1)} %get-tuple-element.9), channel_id=1, source_target_pairs={{0,1},{1,2},{2,3},{3,4},{4,5},{5,6},{6,7},{7,0},{8,9},{9,10},{10,1... | collective-permute-start | bytes 196616 | tf_op jit(solution)/shard_map/ppermute | solution.py:48
  3.6 22.2 %collective-permute-start.11 = (bf16[32,1024]{1,0:T(8,128)(2,1)S(1)}, bf16[32,1024]{1,0:T(8,128)(2,1)S(1)}, u32[]{:S(2)}, u32[]{:S(2)}) collective-permute-start(bf16[32,1024]{1,0:T(8,128)(2,1)S(1)} %get-tuple-element.9), channel_id=1, source_target_pairs={{0,7},{1,0},{2,1},{3,2},{4,3},{5,4},{6,5},{7,6},{8,15},{9,8},{10,9... | collective-permute-start | bytes 196616 | tf_op jit(solution)/shard_map/ppermute | solution.py:51
  4.8 42.3 %collective-permute-start = (bf16[9,4,16]{2,1,0:T(4,128)(2,1)S(1)}, bf16[9,4,16]{2,1,0:T(4,128)(2,1)S(1)}, u32[]{:S(2)}, u32[]{:S(2)}) collective-permute-start(bf16[9,4,16]{2,1,0:T(4,128)(2,1)S(1)} %get-tuple-element.21), channel_id=1, source_target_pairs={{0,32},{32,0},{64,96},{96,64},{128,160},{160,128},{192,224},{224,1... | collective-permute-start | bytes 3464 | tf_op jit(solution)/shard_map/ppermute | solution.py:117
  4.9 42.2 %collective-permute-start.1 = (bf16[9,4,16]{2,1,0:T(4,128)(2,1)S(1)}, bf16[9,4,16]{2,1,0:T(4,128)(2,1)S(1)}, u32[]{:S(2)}, u32[]{:S(2)}) collective-permute-start(bf16[9,4,16]{2,1,0:T(4,128)(2,1)S(1)} %get-tuple-element.20), channel_id=1, source_target_pairs={{0,64},{32,96},{64,0},{96,32},{128,192},{160,224},{192,128},{224,1... | collective-permute-start | bytes 3464 | tf_op jit(solution)/shard_map/ppermute | solution.py:117
  6.6 43.7 %collective-permute-start.2 = (bf16[9,4,16]{2,1,0:T(4,128)(2,1)S(1)}, bf16[9,4,16]{2,1,0:T(4,128)(2,1)S(1)}, u32[]{:S(2)}, u32[]{:S(2)}) collective-permute-start(bf16[9,4,16]{2,1,0:T(4,128)(2,1)S(1)} %get-tuple-element.19), channel_id=1, source_target_pairs={{0,96},{32,64},{64,32},{96,0},{128,224},{160,192},{192,160},{224,1... | collective-permute-start | bytes 3464 | tf_op jit(solution)/shard_map/ppermute | solution.py:117
  7.8 37.9 %copy-start.12 = (bf16[48,1024]{1,0:T(8,128)(2,1)S(1)}, bf16[48,1024]{1,0:T(8,128)(2,1)}, u32[]{:S(2)}) copy-start(bf16[48,1024]{1,0:T(8,128)(2,1)} %param.12) | copy-start | bytes 294916
  9.6 68.2 %all-to-all-start = ((f32[32,1,512]{2,1,0:T(1,128)}), f32[32,1,512]{2,1,0:T(1,128)S(1)}, u32[]{:S(2)}, u32[]{:S(2)}) async-start(f32[32,1,512]{2,1,0:T(1,128)} %reshape.267), calls=%async_computation | async-start | bytes 131072 | tf_op jit(solution)/shard_map/all_to_all | solution.py:96
  24.2 4.3 %collective-permute-start.8 = (bf16[32,1024]{1,0:T(8,128)(2,1)S(1)}, bf16[32,1024]{1,0:T(8,128)(2,1)S(1)}, u32[]{:S(2)}, u32[]{:S(2)}) collective-permute-start(bf16[32,1024]{1,0:T(8,128)(2,1)S(1)} %collective-permute-done.7), channel_id=1, source_target_pairs={{0,1},{1,2},{2,3},{3,4},{4,5},{5,6},{6,7},{7,0},{8,9},{9,10},{10,1... | collective-permute-start | bytes 196616 | tf_op jit(solution)/shard_map/ppermute | solution.py:48
  25.8 8.5 %collective-permute-start.12 = (bf16[32,1024]{1,0:T(8,128)(2,1)S(1)}, bf16[32,1024]{1,0:T(8,128)(2,1)S(1)}, u32[]{:S(2)}, u32[]{:S(2)}) collective-permute-start(bf16[32,1024]{1,0:T(8,128)(2,1)S(1)} %collective-permute-done.11), channel_id=1, source_target_pairs={{0,7},{1,0},{2,1},{3,2},{4,3},{5,4},{6,5},{7,6},{8,15},{9,8},{10,9... | collective-permute-start | bytes 196616 | tf_op jit(solution)/shard_map/ppermute | solution.py:51
  28.6 4.3 %collective-permute-start.9 = (bf16[32,1024]{1,0:T(8,128)(2,1)S(1)}, bf16[32,1024]{1,0:T(8,128)(2,1)S(1)}, u32[]{:S(2)}, u32[]{:S(2)}) collective-permute-start(bf16[32,1024]{1,0:T(8,128)(2,1)S(1)} %collective-permute-done.8), channel_id=1, source_target_pairs={{0,1},{1,2},{2,3},{3,4},{4,5},{5,6},{6,7},{7,0},{8,9},{9,10},{10,1... | collective-permute-start | bytes 196616 | tf_op jit(solution)/shard_map/ppermute | solution.py:48
  32.8 5.0 %collective-permute-start.10 = (bf16[32,1024]{1,0:T(8,128)(2,1)S(1)}, bf16[32,1024]{1,0:T(8,128)(2,1)S(1)}, u32[]{:S(2)}, u32[]{:S(2)}) collective-permute-start(bf16[32,1024]{1,0:T(8,128)(2,1)S(1)} %collective-permute-done.9), channel_id=1, source_target_pairs={{0,1},{1,2},{2,3},{3,4},{4,5},{5,6},{6,7},{7,0},{8,9},{9,10},{10,1... | collective-permute-start | bytes 196616 | tf_op jit(solution)/shard_map/ppermute | solution.py:48
  34.3 21.3 %collective-permute-start.3 = (bf16[9,4,16]{2,1,0:T(4,128)(2,1)S(1)}, bf16[9,4,16]{2,1,0:T(4,128)(2,1)S(1)}, u32[]{:S(2)}, u32[]{:S(2)}) collective-permute-start(bf16[9,4,16]{2,1,0:T(4,128)(2,1)S(1)} %get-tuple-element.18), channel_id=1, source_target_pairs={{0,128},{32,160},{64,192},{96,224},{128,0},{160,32},{192,64},{224,... | collective-permute-start | bytes 3464 | tf_op jit(solution)/shard_map/ppermute | solution.py:117
  37.8 5.1 %collective-permute-start.13 = (bf16[32,1024]{1,0:T(8,128)(2,1)S(1)}, bf16[32,1024]{1,0:T(8,128)(2,1)S(1)}, u32[]{:S(2)}, u32[]{:S(2)}) collective-permute-start(bf16[32,1024]{1,0:T(8,128)(2,1)S(1)} %collective-permute-done.12), channel_id=1, source_target_pairs={{0,7},{1,0},{2,1},{3,2},{4,3},{5,4},{6,5},{7,6},{8,15},{9,8},{10,9... | collective-permute-start | bytes 196616 | tf_op jit(solution)/shard_map/ppermute | solution.py:51
  43.7 11.7 %collective-permute-start.14 = (bf16[8,32,1024]{2,1,0:T(8,128)(2,1)S(1)}, bf16[8,32,1024]{2,1,0:T(8,128)(2,1)S(1)}, u32[]{:S(2)}, u32[]{:S(2)}) collective-permute-start(bf16[8,32,1024]{2,1,0:T(8,128)(2,1)S(1)} %broadcast_select_fusion.6), channel_id=1, source_target_pairs={{0,8},{1,9},{2,10},{3,11},{4,12},{5,13},{6,14},{7,15},{8,16},{9,17... | collective-permute-start | bytes 1572872 | tf_op jit(solution)/shard_map/ppermute | solution.py:48
  45.6 28.4 %copy-start.17 = (pred[48]{0:T(512)(128)(4,1)}, pred[48]{0:T(512)(128)(4,1)S(1)}, u32[]{:S(2)}) copy-start(pred[48]{0:T(512)(128)(4,1)S(1)} %compare_and_fusion.3) | copy-start | bytes 148
  47.1 8.6 %collective-permute-start.4 = (bf16[9,4,16]{2,1,0:T(4,128)(2,1)S(1)}, bf16[9,4,16]{2,1,0:T(4,128)(2,1)S(1)}, u32[]{:S(2)}, u32[]{:S(2)}) collective-permute-start(bf16[9,4,16]{2,1,0:T(4,128)(2,1)S(1)} %get-tuple-element.17), channel_id=1, source_target_pairs={{0,160},{32,128},{64,224},{96,192},{128,32},{160,0},{192,96},{224,... | collective-permute-start | bytes 3464 | tf_op jit(solution)/shard_map/ppermute | solution.py:117
  47.2 26.1 %collective-permute-start.5 = (bf16[9,4,16]{2,1,0:T(4,128)(2,1)S(1)}, bf16[9,4,16]{2,1,0:T(4,128)(2,1)S(1)}, u32[]{:S(2)}, u32[]{:S(2)}) collective-permute-start(bf16[9,4,16]{2,1,0:T(4,128)(2,1)S(1)} %get-tuple-element.23), channel_id=1, source_target_pairs={{0,192},{32,224},{64,128},{96,160},{128,64},{160,96},{192,0},{224,... | collective-permute-start | bytes 3464 | tf_op jit(solution)/shard_map/ppermute | solution.py:117
  50.3 14.8 %collective-permute-start.16 = (bf16[8,32,1024]{2,1,0:T(8,128)(2,1)S(1)}, bf16[8,32,1024]{2,1,0:T(8,128)(2,1)S(1)}, u32[]{:S(2)}, u32[]{:S(2)}) collective-permute-start(bf16[8,32,1024]{2,1,0:T(8,128)(2,1)S(1)} %broadcast_select_fusion.6), channel_id=1, source_target_pairs={{0,24},{1,25},{2,26},{3,27},{4,28},{5,29},{6,30},{7,31},{8,0},{9,1... | collective-permute-start | bytes 1572872 | tf_op jit(solution)/shard_map/ppermute | solution.py:51
  55.4 12.3 %collective-permute-start.15 = (bf16[8,32,1024]{2,1,0:T(8,128)(2,1)S(1)}, bf16[8,32,1024]{2,1,0:T(8,128)(2,1)S(1)}, u32[]{:S(2)}, u32[]{:S(2)}) collective-permute-start(bf16[8,32,1024]{2,1,0:T(8,128)(2,1)S(1)} %collective-permute-done.14), channel_id=1, source_target_pairs={{0,8},{1,9},{2,10},{3,11},{4,12},{5,13},{6,14},{7,15},{8,16},{9,17... | collective-permute-start | bytes 1572872 | tf_op jit(solution)/shard_map/ppermute | solution.py:48
  55.6 17.7 %collective-permute-start.6 = (bf16[9,4,16]{2,1,0:T(4,128)(2,1)S(1)}, bf16[9,4,16]{2,1,0:T(4,128)(2,1)S(1)}, u32[]{:S(2)}, u32[]{:S(2)}) collective-permute-start(bf16[9,4,16]{2,1,0:T(4,128)(2,1)S(1)} %get-tuple-element.16), channel_id=1, source_target_pairs={{0,224},{32,192},{64,160},{96,128},{128,96},{160,64},{192,32},{224... | collective-permute-start | bytes 3464 | tf_op jit(solution)/shard_map/ppermute | solution.py:117
  73.3 15.6 %collective-permute-start.17 = (bf16[1024,1024]{1,0:T(8,128)(2,1)}, bf16[1024,1024]{1,0:T(8,128)(2,1)}, u32[]{:S(2)}, u32[]{:S(2)}) collective-permute-start(bf16[1024,1024]{1,0:T(8,128)(2,1)} %bitcast_select_fusion), channel_id=1, source_target_pairs={{0,32},{32,0},{64,96},{96,64},{128,160},{160,128},{192,224},{224,1... | collective-permute-start | bytes 6291464 | tf_op jit(solution)/shard_map/ppermute | solution.py:101
  74.0 3.8 %copy-start.8 = (bf16[48,4,16]{2,1,0:T(4,128)(2,1)}, bf16[48,4,16]{2,1,0:T(4,128)(2,1)S(1)}, u32[]{:S(2)}) copy-start(bf16[48,4,16]{2,1,0:T(4,128)(2,1)S(1)} %gather_fusion) | copy-start | bytes 18436
  79.5 6.6 %copy-start.1 = (bf16[48,16,1024]{2,1,0:T(8,128)(2,1)S(1)}, bf16[48,16,1024]{2,1,0:T(8,128)(2,1)}, u32[]{:S(2)}) copy-start(bf16[48,16,1024]{2,1,0:T(8,128)(2,1)} %get-tuple-element.13) | copy-start | bytes 4718596
  84.6 4.3 %copy-start.10 = (f32[16,48,16]{1,0,2:T(8,128)}, f32[16,48,16]{1,0,2:T(8,128)S(1)}, u32[]{:S(2)}) copy-start(f32[16,48,16]{1,0,2:T(8,128)S(1)} %get-tuple-element.26) | copy-start | bytes 147460
  84.6 4.3 %copy-start.19 = (bf16[16,1024]{1,0:T(8,128)(2,1)S(1)}, bf16[16,1024]{1,0:T(8,128)(2,1)}, u32[]{:S(2)}) copy-start(bf16[16,1024]{1,0:T(8,128)(2,1)} %param.17) | copy-start | bytes 98308
  84.7 0.7 copy-start.13
  94.4 2.6 %copy-start.2 = (bf16[48,16,1024]{2,1,0:T(8,128)(2,1)S(1)}, bf16[48,16,1024]{2,1,0:T(8,128)(2,1)}, u32[]{:S(2)}) copy-start(bf16[48,16,1024]{2,1,0:T(8,128)(2,1)} %get-tuple-element.13) | copy-start | bytes 4718596
  97.1 1.2 copy-start.11
  97.1 1.2 copy-start.14
  97.1 4.2 %copy-start.7 = (bf16[48,1024]{1,0:T(8,128)(2,1)S(1)}, bf16[48,1024]{1,0:T(8,128)(2,1)}, u32[]{:S(2)}) copy-start(bf16[48,1024]{1,0:T(8,128)(2,1)} %pad_maximum_fusion.2) | copy-start | bytes 294916
  101.4 1.9 %copy-start.3 = (f32[48,16,1024]{2,1,0:T(8,128)S(1)}, f32[48,16,1024]{2,1,0:T(8,128)}, u32[]{:S(2)}) copy-start(f32[48,16,1024]{2,1,0:T(8,128)} %get-tuple-element.12) | copy-start | bytes 9437188
  101.5 1.9 %copy-start.9 = (bf16[48,4,16]{2,1,0:T(4,128)(2,1)S(1)}, bf16[48,4,16]{2,1,0:T(4,128)(2,1)}, u32[]{:S(2)}) copy-start(bf16[48,4,16]{2,1,0:T(4,128)(2,1)} %copy-done.8) | copy-start | bytes 18436
  101.5 1.9 %copy-start.18 = (pred[48]{0:T(512)(128)(4,1)S(1)}, pred[48]{0:T(512)(128)(4,1)}, u32[]{:S(2)}) copy-start(pred[48]{0:T(512)(128)(4,1)} %copy-done.17) | copy-start | bytes 148
  107.9 1.5 copy-start.15
  107.9 1.5 copy-start.16
  109.4 5.5 %copy-start.4 = (bf16[16,16,1024]{2,1,0:T(8,128)(2,1)S(1)}, bf16[16,16,1024]{2,1,0:T(8,128)(2,1)}, u32[]{:S(2)}) copy-start(bf16[16,16,1024]{2,1,0:T(8,128)(2,1)} %get-tuple-element.10) | copy-start | bytes 1572868
  109.4 5.5 %copy-start.5 = (bf16[16,16,1024]{2,1,0:T(8,128)(2,1)S(1)}, bf16[16,16,1024]{2,1,0:T(8,128)(2,1)}, u32[]{:S(2)}) copy-start(bf16[16,16,1024]{2,1,0:T(8,128)(2,1)} %get-tuple-element.11) | copy-start | bytes 1572868
  110.7 21.6 %all-to-all-start.1 = ((f32[8,9,32,128]{3,2,1,0:T(8,128)}), f32[8,9,32,128]{3,2,1,0:T(8,128)}, u32[]{:S(2)}, u32[]{:S(2)}) async-start(f32[8,9,32,128]{3,2,1,0:T(8,128)} %select_select_fusion), calls=%async_computation.1 | async-start | bytes 2359296 | tf_op jit(solution)/shard_map/all_to_all | solution.py:182
  117.8 3.0 %copy-start.6 = (bf16[32,16,1024]{2,1,0:T(8,128)(2,1)S(1)}, bf16[32,16,1024]{2,1,0:T(8,128)(2,1)}, u32[]{:S(2)}) copy-start(bf16[32,16,1024]{2,1,0:T(8,128)(2,1)} %pad_maximum_fusion.1) | copy-start | bytes 3145732
  134.4 21.4 %all-to-all-start.2 = ((f32[32,9,128]{2,1,0:T(8,128)}), f32[32,9,128]{2,1,0:T(8,128)S(1)}, u32[]{:S(2)}, u32[]{:S(2)}) async-start(f32[32,9,128]{2,1,0:T(8,128)} %copy.57), calls=%async_computation.2 | async-start | bytes 524288 | tf_op jit(solution)/shard_map/all_to_all | solution.py:183
